TPU v7x, 256 devices: a whole 4x4x8 slice. The times are simulated.
256 devices in a mesh: aa: 32 (over z, x), ba: 8 (over y, core).
Axes of the slice: x: 4, y: 4, z: 8, core: 2. Of those that a mesh axis runs over, the one named last changes fastest.
Arguments:
- snapshots: float32 [8192, 65536], P(('aa', 'ba')), may hold values from -125 to 125
Outputs:
- factors: float32 [8, 64, 64], replicated
- pod_modes: float32 [8, 64, 65536], P(None, None, ('aa', 'ba'))
All inputs are finite; a program needn't handle non-finite values.
Results may differ from a plain program's by a relative error of at most 0.000098.
Values sent between devices are 32-bit elements; how exact they have to be, the bound alone decides.
No kernel may reach another device: no remote copies, remote signals or barrier semaphores. Data moves between devices by JAX's collectives and lax.ppermute only.
A program may use at most 128 MiB of HBM per device.

v0:
```python
import math
import jax
import jax.numpy as jnp
from jax import lax
from jax.sharding import PartitionSpec as P

FREQS = 8


def spectral_table(block_len, points):
    sample = jnp.arange(block_len, dtype=jnp.int32)
    harmonic = jnp.arange(1, FREQS + 1, dtype=jnp.int32)
    phase_turns = (sample[:, None] * harmonic[None, :] % block_len).astype(jnp.float32) * (
        2.0 * math.pi / block_len
    )
    sample_angle = sample.astype(jnp.float32) * (2.0 * math.pi / block_len)
    window = 0.5 - 0.5 * jnp.cos(sample_angle)
    norm_scale = 1.0 / jnp.sqrt(points * jnp.sum(window * window))
    cosine = window[:, None] * jnp.cos(phase_turns) * norm_scale
    sine = -window[:, None] * jnp.sin(phase_turns) * norm_scale
    return jnp.stack([cosine, sine], axis=1)


def local(snapshots):
    time_dev, points = snapshots.shape
    n_aa = lax.axis_size("aa")
    n_ba = lax.axis_size("ba")
    pts_dev = points // (n_aa * n_ba)
    block_len = time_dev * n_ba
    table = spectral_table(block_len, points)
    regrouped = lax.all_to_all(
        lax.all_to_all(snapshots, "aa", split_axis=1, concat_axis=0, tiled=True),
        "ba",
        split_axis=1,
        concat_axis=0,
        tiled=True,
    )
    arranged = regrouped.reshape(n_ba, n_aa, time_dev, pts_dev)
    table_parts = table.reshape(n_ba, time_dev, 2, FREQS)
    spectra = jnp.einsum("uasp,usgf->agfp", arranged, table_parts, precision=lax.Precision.HIGHEST)
    blocks = spectra.shape[0]
    columns = 2 * blocks
    product = jnp.einsum("bgfp,chfp->fbgch", spectra, spectra, precision=lax.Precision.HIGHEST)
    gram_sum = lax.psum(product.reshape(FREQS, columns, columns), ("aa", "ba"))
    lower_factor = jnp.linalg.cholesky(gram_sum)
    identity = jnp.broadcast_to(jnp.eye(columns, dtype=gram_sum.dtype), lower_factor.shape)
    inverse = lax.linalg.triangular_solve(lower_factor, identity, left_side=True, lower=True)
    pod_modes = math.sqrt(points) * jnp.einsum(
        "fibg,bgfp->fip",
        inverse.reshape(FREQS, columns, blocks, 2),
        spectra,
        precision=lax.Precision.HIGHEST,
    )
    return (jnp.swapaxes(lower_factor, 1, 2), pod_modes)


def solution(mesh):
    placed = (P(("aa", "ba"), None),)
    return jax.shard_map(
        local,
        mesh=mesh,
        in_specs=placed,
        out_specs=(P(), P(None, None, ("aa", "ba"))),
        check_vma=False,
    )
```

profile of v0, /device:TPU:2, one launch (start us, length us, event | category | flops | bytes accessed | tf_op | source)
XLA Modules:
  0.0 675.1 jit_solution(12656147163398301146)
XLA Ops:
  7.2 4.0 copy.75
  11.1 196.8 %all_to_all.32 = f32[32,32,2048]{2,0,1:T(8,128)S(1)} all-to-all(f32[32,32,2048]{2,0,1:T(8,128)S(1)} %bitcast.46), channel_id=1, replica_groups=mesh['aa'=32,'ba'=8] {'aa'}, dimensions={1} | all-to-all | bytes 16777216 | tf_op jit(solution)/shard_map/all_to_all | solution.py:32
  207.9 4.1 copy.61
  212.0 5.8 copy.38
  217.8 5.0 all-to-all-start.1
  222.8 0.2 all-reduce.2.cloned.1.call-start
  223.0 0.6 multiply_reduce_fusion
  224.4 0.2 multiply_multiply_fusion.1
  224.7 92.7 %all-to-all-done.1 = f32[1024,8,256]{2,0,1:T(8,128)} async-done(((f32[1024,8,256]{2,0,1:T(8,128)}), f32[1024,8,256]{2,0,1:T(8,128)}, u32[]{:S(2)}, u32[]{:S(2)}) %all-to-all-start.1) | async-done | bytes 8388640 | tf_op jit(solution)/shard_map/all_to_all | solution.py:31
  317.4 9.1 %fusion = f32[2,8,32,256,1]{3,1,4,2,0:T(8,128)S(1)} fusion(f32[8,32,32,256]{3,2,1,0:T(8,128)} %bitcast.4, f32[8,32,1,8]{1,3,0,2:T(8,128)S(1)} %get-tuple-element.13, f32[8,32,1,8]{1,3,0,2:T(8,128)S(1)} %get-tuple-element.12), kind=kOutput, calls=%fused_computation.1 | convolution fusion | flops 402657280 | bytes 8929280 | tf_op jit(solution)/shard_map/uasp,usgf->agfp/dot_general | solution.py:40
  326.5 1.6 fusion.4
  328.1 1.2 copy.42
  329.3 1.9 copy.43
  331.2 0.0 all-reduce.2.cloned.1.call-update
  331.3 245.3 %all-reduce.2.cloned.1.call-done = f32[8,64,64]{1,2,0:T(8,128)} async-done(((f32[8,64,64]{1,2,0:T(8,128)}), f32[8,64,64]{1,2,0:T(8,128)}) %all-reduce.2.cloned.1.call-update) | async-done | bytes 131088 | tf_op jit(solution)/shard_map/psum | solution.py:44
  576.5 1.1 copy.44
  577.6 1.0 fusion.10
  578.6 46.9 %custom-call.7 = f32[8,64,64]{2,1,0:T(8,128)S(1)} custom-call(f32[8,64,64]{2,1,0:T(8,128)S(1)} %fusion.10), custom_call_target="Cholesky" | custom-call | tf_op jit(solution)/shard_map/jit(cholesky)/cholesky | solution.py:45
  625.5 0.1 compare_reduce_fusion
  625.7 0.1 select_bitcast_fusion
  625.8 0.8 copy.49
  626.6 39.3 %custom-call.8 = f32[8,1,64,64]{2,3,1,0:T(8,128)S(1)} custom-call(f32[8,1,64,64]{3,2,1,0:T(8,128)S(1)} %get-tuple-element.10), custom_call_target="InvertDiagBlocksLowerTriangular" | custom-call | tf_op jit(solution)/shard_map/triangular_solve | solution.py:47
  665.9 0.6 fusion.8
  666.5 0.1 copy.46
  666.7 1.6 fusion.3
  (7 shorter events, 0.1 us)
Async XLA Ops:
  217.8 99.6 %all-to-all-start.1 = ((f32[1024,8,256]{2,0,1:T(8,128)}), f32[1024,8,256]{2,0,1:T(8,128)}, u32[]{:S(2)}, u32[]{:S(2)}) async-start(f32[1024,8,256]{2,0,1:T(8,128)} %copy.38), calls=%async_computation.1 | async-start | bytes 16777216 | tf_op jit(solution)/shard_map/all_to_all | solution.py:31
  222.8 353.8 %all-reduce.2.cloned.1.call-start = ((), (), s32[]{:S(2)}) async-start(), calls=%async_computation.2 | async-start | bytes 524288 | tf_op jit(solution)/shard_map/psum | solution.py:44
Sparse Core Ops, SparseCore 0:
  331.4 245.1 all-reduce.1
where the time goes:
time: 675 us
  waiting for transfers between devices  338 us (50%)
  blocking collectives  197 us (29%)
  other arithmetic  88.4 us (13%)
  local copies, waits for them, and re-layouts  19 us (3%)
  between operations  14.8 us (2%)
  matrix products  12.9 us (2%)
    psum x1, waiting for transfers between devices, local(): gram_sum = lax.psum(product.reshape(FREQS, columns, columns), ('aa', 'ba'))  245 us
    all_to_all x1, blocking collectives, local(): lax.all_to_all(snapshots, 'aa', split_axis=1, concat_axis=0, tiled=True)  197 us
    all_to_all x1, waiting for transfers between devices, local(): lax.all_to_all(lax.all_to_all(snapshots, 'aa', split_axis=1, concat_axis=...  92.7 us
    another operation x4, other arithmetic, local(): lower_factor = jnp.linalg.cholesky(gram_sum)  47.1 us
    another operation x2, other arithmetic, local(): lax.linalg.triangular_solve(lower_factor, identity, left_side=True, lower...  39.4 us
  transfers between devices with their start and end apart: 2, of which 2 were waited for; matrix products, arithmetic and copies ran while one was open for 0% of the time, Pallas kernels for 0%

commit v1 on v0

--- a/solution.py
+++ b/solution.py
@@ -41,7 +41,7 @@
     blocks = spectra.shape[0]
     columns = 2 * blocks
     product = jnp.einsum("bgfp,chfp->fbgch", spectra, spectra, precision=lax.Precision.HIGHEST)
-    gram_sum = lax.psum(product.reshape(FREQS, columns, columns), ("aa", "ba"))
+    gram_sum = lax.psum(lax.psum(product.reshape(FREQS, columns, columns), "aa"), "ba")
     lower_factor = jnp.linalg.cholesky(gram_sum)
     identity = jnp.broadcast_to(jnp.eye(columns, dtype=gram_sum.dtype), lower_factor.shape)
     inverse = lax.linalg.triangular_solve(lower_factor, identity, left_side=True, lower=True)

time: 675 us -> 634 us (0.939)
  waiting for transfers between devices: 338 us -> 296 us
    psum x1 -> x2, waiting for transfers between devices: 245 us -> 203 us  [the longest x1 138 us: local(): lax.psum(product.reshape(FREQS, columns, columns), 'aa')]
  transfers between devices with their start and end apart: 2 -> 3, of which waited for: 2 -> 3; matrix products, arithmetic and copies ran while one was open for 0% -> 0% of each run, Pallas kernels for 0% -> 0%
where the time goes in v1:
time: 634 us; the launch traced here: 633 us
  waiting for transfers between devices  296 us (47%)
  blocking collectives  197 us (31%)
  other arithmetic  88.4 us (14%)
  local copies, waits for them, and re-layouts  19 us (3%)
  between operations  14.8 us (2%)
  matrix products  12.9 us (2%)
    all_to_all x1, blocking collectives, local(): lax.all_to_all(snapshots, 'aa', split_axis=1, concat_axis=0, tiled=True)  197 us
    psum x1, waiting for transfers between devices, local(): lax.psum(product.reshape(FREQS, columns, columns), 'aa')  138 us
    all_to_all x1, waiting for transfers between devices, local(): lax.all_to_all(lax.all_to_all(snapshots, 'aa', split_axis=1, concat_axis=...  92.7 us
    psum x1, waiting for transfers between devices, local(): lax.psum(lax.psum(product.reshape(FREQS, columns, columns), 'aa'), 'ba')  65.4 us
    another operation x4, other arithmetic, local(): lower_factor = jnp.linalg.cholesky(gram_sum)  47.1 us
    another operation x2, other arithmetic, local(): lax.linalg.triangular_solve(lower_factor, identity, left_side=True, lower...  39.4 us
  transfers between devices with their start and end apart: 3, of which 3 were waited for; matrix products, arithmetic and copies ran while one was open for 0% of the time, Pallas kernels for 0%

profile of v1, /device:TPU:2, one launch (start us, length us, event | category | flops | bytes accessed | tf_op | source)
XLA Modules:
  0.0 633.2 jit_solution(1364482919001259132)
XLA Ops:
  7.2 4.0 copy.75
  11.1 196.8 %all_to_all.32 = f32[32,32,2048]{2,0,1:T(8,128)S(1)} all-to-all(f32[32,32,2048]{2,0,1:T(8,128)S(1)} %bitcast.46), channel_id=1, replica_groups=mesh['aa'=32,'ba'=8] {'aa'}, dimensions={1} | all-to-all | bytes 16777216 | tf_op jit(solution)/shard_map/all_to_all | solution.py:32
  207.9 4.1 copy.61
  212.0 5.8 copy.38
  217.8 5.0 all-to-all-start.1
  222.8 0.2 all-reduce.3.cloned.1.call-start
  223.0 0.6 multiply_reduce_fusion
  224.4 0.2 multiply_multiply_fusion.1
  224.6 92.7 %all-to-all-done.1 = f32[1024,8,256]{2,0,1:T(8,128)} async-done(((f32[1024,8,256]{2,0,1:T(8,128)}), f32[1024,8,256]{2,0,1:T(8,128)}, u32[]{:S(2)}, u32[]{:S(2)}) %all-to-all-start.1) | async-done | bytes 8388640 | tf_op jit(solution)/shard_map/all_to_all | solution.py:31
  317.4 9.1 %fusion = f32[2,8,32,256,1]{3,1,4,2,0:T(8,128)S(1)} fusion(f32[8,32,32,256]{3,2,1,0:T(8,128)} %bitcast.4, f32[8,32,1,8]{1,3,0,2:T(8,128)S(1)} %get-tuple-element.13, f32[8,32,1,8]{1,3,0,2:T(8,128)S(1)} %get-tuple-element.12), kind=kOutput, calls=%fused_computation.1 | convolution fusion | flops 402657280 | bytes 8929280 | tf_op jit(solution)/shard_map/uasp,usgf->agfp/dot_general | solution.py:40
  326.5 1.6 fusion.4
  328.1 1.2 copy.42
  329.3 1.9 copy.43
  331.2 0.0 all-reduce.3.cloned.1.call-update
  331.2 0.0 all-reduce.5.cloned.1.call-start
  331.3 137.8 %all-reduce.3.cloned.1.call-done = f32[8,64,64]{1,2,0:T(8,128)} async-done(((f32[8,64,64]{1,2,0:T(8,128)}), f32[8,64,64]{1,2,0:T(8,128)}) %all-reduce.3.cloned.1.call-update) | async-done | bytes 131088 | tf_op jit(solution)/shard_map/psum | solution.py:44
  469.2 0.0 all-reduce.5.cloned.1.call-update
  469.2 65.4 %all-reduce.5.cloned.1.call-done = f32[8,64,64]{1,2,0:T(8,128)} async-done(((f32[8,64,64]{1,2,0:T(8,128)}), f32[8,64,64]{1,2,0:T(8,128)}) %all-reduce.5.cloned.1.call-update) | async-done | bytes 131088 | tf_op jit(solution)/shard_map/psum | solution.py:44
  534.6 1.1 copy.44
  535.7 1.0 fusion.10
  536.7 46.9 %custom-call.7 = f32[8,64,64]{2,1,0:T(8,128)S(1)} custom-call(f32[8,64,64]{2,1,0:T(8,128)S(1)} %fusion.10), custom_call_target="Cholesky" | custom-call | tf_op jit(solution)/shard_map/jit(cholesky)/cholesky | solution.py:45
  583.6 0.1 compare_reduce_fusion
  583.8 0.1 select_bitcast_fusion
  583.9 0.8 copy.49
  584.7 39.3 %custom-call.8 = f32[8,1,64,64]{2,3,1,0:T(8,128)S(1)} custom-call(f32[8,1,64,64]{3,2,1,0:T(8,128)S(1)} %get-tuple-element.10), custom_call_target="InvertDiagBlocksLowerTriangular" | custom-call | tf_op jit(solution)/shard_map/triangular_solve | solution.py:47
  624.0 0.6 fusion.8
  624.6 0.1 copy.46
  624.8 1.6 fusion.3
  (7 shorter events, 0.1 us)
Async XLA Ops:
  217.8 99.6 %all-to-all-start.1 = ((f32[1024,8,256]{2,0,1:T(8,128)}), f32[1024,8,256]{2,0,1:T(8,128)}, u32[]{:S(2)}, u32[]{:S(2)}) async-start(f32[1024,8,256]{2,0,1:T(8,128)} %copy.38), calls=%async_computation.1 | async-start | bytes 16777216 | tf_op jit(solution)/shard_map/all_to_all | solution.py:31
  222.8 246.4 %all-reduce.3.cloned.1.call-start = ((), (), s32[]{:S(2)}) async-start(), calls=%async_computation.2 | async-start | bytes 524288 | tf_op jit(solution)/shard_map/psum | solution.py:44
  331.2 203.4 %all-reduce.5.cloned.1.call-start = ((), (), s32[]{:S(2)}) async-start(), calls=%async_computation.3 | async-start | bytes 524288 | tf_op jit(solution)/shard_map/psum | solution.py:44
Sparse Core Ops, SparseCore 0:
  331.4 137.7 all-reduce.2
  471.5 63.1 all-reduce.4
